TPU v7x, 32 devices: a whole 2x2x4 slice. The times are simulated.
32 devices in a mesh: groups: 1, gx: 32 (over z, y, x, core).
Axes of the slice: x: 2, y: 2, z: 4, core: 2. Of those that a mesh axis runs over, the one named last changes fastest.
Arguments:
- solid_state: float32 [9, 2, 1, 256, 4, 128], P(None, None, 'groups', 'gx'), may hold values from -6 to 6
- water_state: float32 [4, 2, 1, 128, 12, 256], P(None, None, 'groups', 'gx'), may hold values from -6 to 6
- lame_lambda: float32 [256, 4, 128], P('gx'), may hold values from 0.4 to 1.2
- shear_mu: float32 [256, 4, 128], P('gx'), may hold values from 0.1 to 0.5
- solid_buoy: float32 [256, 4, 128], P('gx'), may hold values from 0.4 to 1
- water_kappa: float32 [128, 12, 256], P('gx'), may hold values from 0.5 to 1
- water_buoy: float32 [128, 12, 256], P('gx'), may hold values from 0.6 to 1.2
- seafloor: int32 [128, 256], P('gx'), may hold values from 6 to 12
- source_cell: int32 [1], P('groups'), may hold values from 0 to 196607
- wavelet: float32 [4, 1], P(None, 'groups'), may hold values from -48 to 48
- receiver_column: int32 [128], replicated, may hold values from 0 to 32767
- observed: float32 [4, 1, 128], P(None, 'groups'), may hold values from -6 to 6
Outputs:
- grad_lambda: float32 [256, 4, 128], P('gx', 'groups')
- grad_mu: float32 [256, 4, 128], P('gx', 'groups')
- grad_kappa: float32 [128, 12, 256], P('gx', 'groups')
- residuals: float32 [4, 1, 128], P(None, 'groups')
Inputs may be any that keep to these rules, and one draw needn't show every extreme that they name: Every column holds water from z = 0 to z = seafloor - 1 and rock below it. source_cell is (z * 128 + y) * 256 + x of a water cell with z below 6. receiver_column is y * 256 + x; two nodes may share a column.
All inputs are finite; a program needn't handle non-finite values.
Results may differ from a plain program's by a relative error of at most 0.00014.
Values sent between devices are 32-bit elements; how exact they have to be, the bound alone decides.
No kernel may reach another device: no remote copies, remote signals or barrier semaphores. Data moves between devices by JAX's collectives and lax.ppermute only.
A program may use at most 64 MiB of HBM per device.

v0:
```python
import jax
import jax.numpy as jnp
from jax import lax
from jax.sharding import PartitionSpec as P

COEFF = (1225.0 / 1024.0, -245.0 / 3072.0, 49.0 / 5120.0, -5.0 / 7168.0)
TIME_STEP = 0.2


def with_halo(array, sides, width):
    for axis, dim in sides:
        devices, length = (lax.axis_size(axis), array.shape[dim])
        up = [(i, (i + 1) % devices) for i in range(devices - 1)]
        down = [(j, i) for i, j in up]
        last = lax.slice_in_dim(array, length - width, length, axis=dim)
        first = lax.slice_in_dim(array, 0, width, axis=dim)
        before = lax.ppermute(last, axis, up)
        after = lax.ppermute(first, axis, down)
        array = jnp.concatenate([before, array, after], axis=dim)
    return array


def stencil(padded, axis, forward):
    length = padded.shape[axis] - 8
    summed = None
    for offset in range(1, 5):
        if forward:
            front_at, back_at = (4 + offset, 5 - offset)
        else:
            front_at, back_at = (3 + offset, 4 - offset)
        front = lax.slice_in_dim(padded, front_at, front_at + length, axis=axis)
        back = lax.slice_in_dim(padded, back_at, back_at + length, axis=axis)
        addend = COEFF[offset - 1] * (front - back)
        summed = addend if summed is None else summed + addend
    return summed


def padded_zero(field, axis):
    widths = [(0, 0)] * field.ndim
    widths[axis] = (4, 4)
    return jnp.pad(field, widths)


def derive(field, axis, forward):
    return stencil(padded_zero(field, axis), axis, forward)


def on_device(
    solid_state,
    water_state,
    lame_lambda,
    shear_mu,
    solid_buoy,
    water_kappa,
    water_buoy,
    seafloor,
    source_cell,
    wavelet,
    receiver_column,
    observed,
):
    parts = lax.axis_size("gx")
    place = lax.axis_index("gx")
    width_x = solid_state.shape[3]
    total_y = solid_state.shape[5]
    total_x = width_x * parts
    shots = solid_state.shape[2]
    shard_axis = 2
    anchor_y = place * water_state.shape[3]
    anchor_x = 0

    def water_halo(field):
        return with_halo(field, (("gx", 2),), 4)

    def water_derive(field, axis, forward):
        if axis == shard_axis:
            return stencil(water_halo(field), axis, forward)
        return derive(field, axis, forward)

    def solid_halo(stacked):
        return with_halo(stacked, (("gx", 3),), 4)

    vel_x, vel_y, vel_z = (solid_state[0], solid_state[1], solid_state[2])
    sig_xx, sig_yy, sig_zz = (solid_state[3], solid_state[4], solid_state[5])
    sig_xy, sig_xz, sig_yz = (solid_state[6], solid_state[7], solid_state[8])
    pressure, flow_x, flow_y, flow_z = (
        water_state[0],
        water_state[1],
        water_state[2],
        water_state[3],
    )
    local_y = pressure.shape[2]
    depth_rows = pressure.shape[3]
    local_x = pressure.shape[4]
    depth_idx = lax.broadcasted_iota(jnp.int32, (1, depth_rows, 1), 1)
    floor_rows = seafloor[:, None, :]
    live = (depth_idx < floor_rows).astype(jnp.float32)
    bottom = (depth_idx == floor_rows - 1).astype(jnp.float32)
    above = (depth_idx < floor_rows - 1).astype(jnp.float32)
    rows_y = lax.broadcasted_iota(jnp.int32, (local_y, 1, 1), 0) + anchor_y
    cols_x = lax.broadcasted_iota(jnp.int32, (1, 1, local_x), 2) + anchor_x
    flat_cell = (depth_idx * total_y + rows_y) * total_x + cols_x
    source_hot = (flat_cell[None] == source_cell[:, None, None, None]).astype(jnp.float32)
    node_y = receiver_column // total_x
    node_x = receiver_column % total_x
    inside = (
        (node_y >= anchor_y)
        & (node_y < anchor_y + local_y)
        & (node_x >= anchor_x)
        & (node_x < anchor_x + local_x)
    )
    local_col = (node_y - anchor_y) * local_x + (node_x - anchor_x)
    column_iota = lax.broadcasted_iota(jnp.int32, (1, local_y * local_x), 1)
    node_hot = ((column_iota == local_col[:, None]) & inside[:, None]).astype(jnp.float32)
    grad_lambda = jnp.zeros(lame_lambda.shape, jnp.float32)
    grad_mu = jnp.zeros(lame_lambda.shape, jnp.float32)
    grad_kappa = jnp.zeros(water_kappa.shape, jnp.float32)
    misfits = []
    for step in range(wavelet.shape[0]):
        floor_pressure = jnp.sum(pressure * bottom, axis=3)
        stress_pad = solid_halo(jnp.stack([sig_xx, sig_xy, sig_xz]))
        vel_x = vel_x + TIME_STEP * solid_buoy * (
            stencil(stress_pad[0], 2, True) + derive(sig_xy, 4, False) + derive(sig_xz, 3, False)
        )
        vel_y = vel_y + TIME_STEP * solid_buoy * (
            stencil(stress_pad[1], 2, False) + derive(sig_yy, 4, True) + derive(sig_yz, 3, False)
        )
        vel_z = vel_z + TIME_STEP * solid_buoy * (
            stencil(stress_pad[2], 2, False) + derive(sig_yz, 4, False) + derive(sig_zz, 3, True)
        )
        floor_velocity = lax.all_to_all(
            jnp.transpose(vel_z[:, :, :, 0, :], (0, 1, 3, 2)),
            "gx",
            split_axis=2,
            concat_axis=3,
            tiled=True,
        )
        flow_x = (flow_x - TIME_STEP * water_buoy * water_derive(pressure, 4, True)) * live
        flow_y = (flow_y - TIME_STEP * water_buoy * water_derive(pressure, 2, True)) * live
        flow_z = (
            flow_z - TIME_STEP * water_buoy * derive(pressure, 3, True)
        ) * above + floor_velocity[:, :, :, None, :] * bottom
        velocity_pad = solid_halo(jnp.stack([vel_x, vel_y, vel_z]))
        strain_x = stencil(velocity_pad[0], 2, False)
        strain_y = derive(vel_y, 4, False)
        strain_z = derive(vel_z, 3, False)
        dilation = strain_x + strain_y + strain_z
        shear_xy = derive(vel_x, 4, True) + stencil(velocity_pad[1], 2, True)
        shear_xz = derive(vel_x, 3, True) + stencil(velocity_pad[2], 2, True)
        shear_yz = derive(vel_y, 3, True) + derive(vel_z, 4, True)
        lam_part = lame_lambda * dilation
        sig_xx = sig_xx + TIME_STEP * (lam_part + 2.0 * shear_mu * strain_x)
        sig_yy = sig_yy + TIME_STEP * (lam_part + 2.0 * shear_mu * strain_y)
        sig_zz = sig_zz + TIME_STEP * (lam_part + 2.0 * shear_mu * strain_z)
        sig_xy = sig_xy + TIME_STEP * shear_mu * shear_xy
        sig_xz = sig_xz + TIME_STEP * shear_mu * shear_xz
        sig_yz = sig_yz + TIME_STEP * shear_mu * shear_yz
        rock_pressure = jnp.transpose(
            lax.all_to_all(floor_pressure, "gx", split_axis=3, concat_axis=2, tiled=True),
            (0, 1, 3, 2),
        )
        sig_zz = sig_zz.at[:, :, :, 0, :].set(-rock_pressure)
        grad_lambda = grad_lambda + jnp.sum(dilation[0] * dilation[1], axis=0)
        normal_part = (
            strain_x[0] * strain_x[1] + strain_y[0] * strain_y[1] + strain_z[0] * strain_z[1]
        )
        shear_part = (
            shear_xy[0] * shear_xy[1] + shear_xz[0] * shear_xz[1] + shear_yz[0] * shear_yz[1]
        )
        grad_mu = grad_mu + jnp.sum(2.0 * normal_part + shear_part, axis=0)
        pressure = (
            pressure
            - TIME_STEP
            * water_kappa
            * (
                water_derive(flow_x, 4, False)
                + water_derive(flow_y, 2, False)
                + derive(flow_z, 3, False)
            )
        ) * live
        pressure = pressure.at[0].add(wavelet[step][:, None, None, None] * source_hot)
        surface = jnp.sum(pressure * bottom, axis=3)
        partial_record = jnp.einsum(
            "sc,rc->sr",
            surface[0].reshape(shots, local_y * local_x),
            node_hot,
            precision=lax.Precision.HIGHEST,
        )
        recorded = lax.psum(partial_record, "gx")
        misfit = recorded - observed[step]
        scaled = misfit * lax.rsqrt(jnp.mean(misfit * misfit, axis=1, keepdims=True) + 1e-06)
        inject = jnp.dot(
            scaled, node_hot, precision=lax.Precision.HIGHEST, preferred_element_type=jnp.float32
        ).reshape(shots, local_y, local_x)
        pressure = pressure.at[1].add(inject[:, :, None, :] * bottom)
        grad_kappa = grad_kappa + jnp.sum(pressure[0] * pressure[1], axis=0)
        misfits.append(misfit)
    return (grad_lambda, grad_mu, grad_kappa, jnp.stack(misfits))


def solution(mesh):
    placed = (
        P(None, None, "groups", "gx", None, None),
        P(None, None, "groups", "gx", None, None),
        P("gx", None, None),
        P("gx", None, None),
        P("gx", None, None),
        P("gx", None, None),
        P("gx", None, None),
        P("gx", None),
        P("groups"),
        P(None, "groups"),
        P(),
        P(None, "groups", None),
    )
    return jax.shard_map(
        on_device,
        mesh=mesh,
        in_specs=placed,
        out_specs=(
            P("gx", "groups", None),
            P("gx", "groups", None),
            P("gx", "groups", None),
            P(None, "groups", None),
        ),
        check_vma=False,
    )
```

profile of v0, /device:TPU:0, one launch (start us, length us, event | category | flops | bytes accessed | tf_op | source)
XLA Modules:
  0.0 367.0 jit_solution(11349562170741559003)
XLA Ops:
  2.9 3.0 collective-permute-start.11
  8.1 5.1 %collective-permute-start = (f32[3,2,1,4,4,128]{5,4,3,2,1,0:T(4,128)S(1)}, f32[3,2,1,4,4,128]{5,4,3,2,1,0:T(4,128)S(1)}, u32[]{:S(2)}, u32[]{:S(2)}) collective-permute-start(f32[3,2,1,4,4,128]{5,4,3,2,1,0:T(4,128)S(1)} %get-tuple-element.248), channel_id=1, source_target_pairs={{0,1},{1,2},{2,3},{3,4},{4,5},{5,6},{6,7},{7,8},{8,9},{9,10},{10,1... | collective-permute-start | bytes 147464 | tf_op jit(solution)/shard_map/ppermute | solution.py:17
  19.5 9.7 %all-to-all-start.1 = ((f32[2,1,128,8]{3,0,1,2:T(2,128)}), f32[2,1,128,8]{3,0,1,2:T(2,128)S(1)}, u32[]{:S(2)}, u32[]{:S(2)}) async-start(f32[2,1,128,8]{3,0,1,2:T(2,128)} %copy.963), calls=%async_computation.1 | async-start | bytes 262144 | tf_op jit(solution)/shard_map/all_to_all | solution.py:131
  31.2 3.0 collective-permute-start.2
  34.2 3.3 all-to-all-done.1
  43.9 3.4 collective-permute-start.12
  52.6 12.4 %all-to-all-start = ((f32[2,1,4,256]{2,0,1,3:T(2,128)}), f32[2,1,4,256]{2,0,1,3:T(2,128)S(1)}, u32[]{:S(2)}, u32[]{:S(2)}) async-start(f32[2,1,4,256]{2,0,1,3:T(2,128)} %copy.948), calls=%async_computation | async-start | bytes 524288 | tf_op jit(solution)/shard_map/all_to_all | solution.py:159
  65.5 40.5 %psum.28 = f32[1,128]{1,0:T(1,128)S(1)} all-reduce(f32[1,128]{1,0:T(1,128)S(1)} %fusion.7), channel_id=1, replica_groups=mesh['groups'=1,'gx'=32] {'gx'}, use_global_device_ids=true, to_apply=%region_2.3 | all-reduce | flops 128 | bytes 1024 | tf_op jit(solution)/shard_map/psum | solution.py:189
  109.1 3.0 collective-permute-start.19
  113.6 6.2 %all-to-all-start.3 = ((f32[2,1,128,8]{3,0,1,2:T(2,128)}), f32[2,1,128,8]{3,0,1,2:T(2,128)S(1)}, u32[]{:S(2)}, u32[]{:S(2)}) async-start(f32[2,1,128,8]{3,0,1,2:T(2,128)} %copy.978), calls=%async_computation.3 | async-start | bytes 262144 | tf_op jit(solution)/shard_map/all_to_all | solution.py:131
  124.2 3.8 %all-to-all-done.3 = f32[2,1,128,8]{3,0,1,2:T(2,128)S(1)} async-done(((f32[2,1,128,8]{3,0,1,2:T(2,128)}), f32[2,1,128,8]{3,0,1,2:T(2,128)S(1)}, u32[]{:S(2)}, u32[]{:S(2)}) %all-to-all-start.3) | async-done | bytes 8224 | tf_op jit(solution)/shard_map/all_to_all | solution.py:131
  133.9 3.4 collective-permute-start.20
  142.7 11.9 %all-to-all-start.2 = ((f32[2,1,4,256]{2,0,1,3:T(2,128)}), f32[2,1,4,256]{2,0,1,3:T(2,128)S(1)}, u32[]{:S(2)}, u32[]{:S(2)}) async-start(f32[2,1,4,256]{2,0,1,3:T(2,128)} %copy.966), calls=%async_computation.2 | async-start | bytes 524288 | tf_op jit(solution)/shard_map/all_to_all | solution.py:159
  155.0 40.5 %psum.29 = f32[1,128]{1,0:T(1,128)S(1)} all-reduce(f32[1,128]{1,0:T(1,128)S(1)} %fusion.5), channel_id=1, replica_groups=mesh['groups'=1,'gx'=32] {'gx'}, use_global_device_ids=true, to_apply=%region_6.7 | all-reduce | flops 128 | bytes 1024 | tf_op jit(solution)/shard_map/psum | solution.py:189
  198.6 3.0 collective-permute-start.25
  203.1 6.2 %all-to-all-start.5 = ((f32[2,1,128,8]{3,0,1,2:T(2,128)}), f32[2,1,128,8]{3,0,1,2:T(2,128)S(1)}, u32[]{:S(2)}, u32[]{:S(2)}) async-start(f32[2,1,128,8]{3,0,1,2:T(2,128)} %copy.989), calls=%async_computation.5 | async-start | bytes 262144 | tf_op jit(solution)/shard_map/all_to_all | solution.py:131
  213.7 3.8 %all-to-all-done.5 = f32[2,1,128,8]{3,0,1,2:T(2,128)S(1)} async-done(((f32[2,1,128,8]{3,0,1,2:T(2,128)}), f32[2,1,128,8]{3,0,1,2:T(2,128)S(1)}, u32[]{:S(2)}, u32[]{:S(2)}) %all-to-all-start.5) | async-done | bytes 8224 | tf_op jit(solution)/shard_map/all_to_all | solution.py:131
  223.4 3.4 collective-permute-start.26
  232.2 11.9 %all-to-all-start.4 = ((f32[2,1,4,256]{2,0,1,3:T(2,128)}), f32[2,1,4,256]{2,0,1,3:T(2,128)S(1)}, u32[]{:S(2)}, u32[]{:S(2)}) async-start(f32[2,1,4,256]{2,0,1,3:T(2,128)} %copy.981), calls=%async_computation.4 | async-start | bytes 524288 | tf_op jit(solution)/shard_map/all_to_all | solution.py:159
  244.5 40.5 %psum.30 = f32[1,128]{1,0:T(1,128)S(1)} all-reduce(f32[1,128]{1,0:T(1,128)S(1)} %fusion.3), channel_id=1, replica_groups=mesh['groups'=1,'gx'=32] {'gx'}, use_global_device_ids=true, to_apply=%region_10.11 | all-reduce | flops 128 | bytes 1024 | tf_op jit(solution)/shard_map/psum | solution.py:189
  288.1 3.0 collective-permute-start.29
  292.6 6.2 %all-to-all-start.6 = ((f32[2,1,128,8]{3,0,1,2:T(2,128)}), f32[2,1,128,8]{3,0,1,2:T(2,128)S(1)}, u32[]{:S(2)}, u32[]{:S(2)}) async-start(f32[2,1,128,8]{3,0,1,2:T(2,128)} %copy.992), calls=%async_computation.6 | async-start | bytes 262144 | tf_op jit(solution)/shard_map/all_to_all | solution.py:131
  303.2 3.8 %all-to-all-done.6 = f32[2,1,128,8]{3,0,1,2:T(2,128)S(1)} async-done(((f32[2,1,128,8]{3,0,1,2:T(2,128)}), f32[2,1,128,8]{3,0,1,2:T(2,128)S(1)}, u32[]{:S(2)}, u32[]{:S(2)}) %all-to-all-start.6) | async-done | bytes 8224 | tf_op jit(solution)/shard_map/all_to_all | solution.py:131
  316.8 46.5 %psum.31 = f32[1,128]{1,0:T(1,128)S(1)} all-reduce(f32[1,128]{1,0:T(1,128)S(1)} %fusion.1), channel_id=1, replica_groups=mesh['groups'=1,'gx'=32] {'gx'}, use_global_device_ids=true, to_apply=%region_13.14 | all-reduce | flops 128 | bytes 1024 | tf_op jit(solution)/shard_map/psum | solution.py:189
  (250 shorter events, 84.0 us)
Async XLA Ops:
  1.6 41.8 %collective-permute-start.10 = (f32[2,1,4,12,256]{4,2,3,1,0:T(4,128)S(1)}, f32[2,1,4,12,256]{4,2,3,1,0:T(4,128)S(1)}, u32[]{:S(2)}, u32[]{:S(2)}) collective-permute-start(f32[2,1,4,12,256]{4,2,3,1,0:T(4,128)S(1)} %slice_bitcast_fusion.3), channel_id=1, source_target_pairs={{1,0},{2,1},{3,2},{4,3},{5,4},{6,5},{7,6},{8,7},{9,8},{10,9},{11,1... | collective-permute-start | bytes 294920 | tf_op jit(solution)/shard_map/ppermute | solution.py:18
  2.9 40.5 %collective-permute-start.11 = (f32[2,1,4,12,256]{4,2,3,1,0:T(4,128)S(1)}, f32[2,1,4,12,256]{4,2,3,1,0:T(4,128)S(1)}, u32[]{:S(2)}, u32[]{:S(2)}) collective-permute-start(f32[2,1,4,12,256]{4,2,3,1,0:T(4,128)S(1)} %slice_bitcast_fusion.3), channel_id=1, source_target_pairs={{0,1},{1,2},{2,3},{3,4},{4,5},{5,6},{6,7},{7,8},{8,9},{9,10},{10,1... | collective-permute-start | bytes 294920 | tf_op jit(solution)/shard_map/ppermute | solution.py:17
  6.8 11.5 %collective-permute-start.1 = (f32[3,2,1,4,4,128]{5,4,3,2,1,0:T(4,128)S(1)}, f32[3,2,1,4,4,128]{5,4,3,2,1,0:T(4,128)S(1)}, u32[]{:S(2)}, u32[]{:S(2)}) collective-permute-start(f32[3,2,1,4,4,128]{5,4,3,2,1,0:T(4,128)S(1)} %get-tuple-element.249), channel_id=1, source_target_pairs={{1,0},{2,1},{3,2},{4,3},{5,4},{6,5},{7,6},{8,7},{9,8},{10,9},{11,1... | collective-permute-start | bytes 147464 | tf_op jit(solution)/shard_map/ppermute | solution.py:18
  8.1 10.3 %collective-permute-start = (f32[3,2,1,4,4,128]{5,4,3,2,1,0:T(4,128)S(1)}, f32[3,2,1,4,4,128]{5,4,3,2,1,0:T(4,128)S(1)}, u32[]{:S(2)}, u32[]{:S(2)}) collective-permute-start(f32[3,2,1,4,4,128]{5,4,3,2,1,0:T(4,128)S(1)} %get-tuple-element.248), channel_id=1, source_target_pairs={{0,1},{1,2},{2,3},{3,4},{4,5},{5,6},{6,7},{7,8},{8,9},{9,10},{10,1... | collective-permute-start | bytes 147464 | tf_op jit(solution)/shard_map/ppermute | solution.py:17
  19.5 18.0 %all-to-all-start.1 = ((f32[2,1,128,8]{3,0,1,2:T(2,128)}), f32[2,1,128,8]{3,0,1,2:T(2,128)S(1)}, u32[]{:S(2)}, u32[]{:S(2)}) async-start(f32[2,1,128,8]{3,0,1,2:T(2,128)} %copy.963), calls=%async_computation.1 | async-start | bytes 262144 | tf_op jit(solution)/shard_map/all_to_all | solution.py:131
  39.1 9.5 %collective-permute-start.5 = (f32[3,2,1,4,4,128]{5,4,3,2,1,0:T(4,128)S(1)}, f32[3,2,1,4,4,128]{5,4,3,2,1,0:T(4,128)S(1)}, u32[]{:S(2)}, u32[]{:S(2)}) collective-permute-start(f32[3,2,1,4,4,128]{5,4,3,2,1,0:T(4,128)S(1)} %get-tuple-element.245), channel_id=1, source_target_pairs={{1,0},{2,1},{3,2},{4,3},{5,4},{6,5},{7,6},{8,7},{9,8},{10,9},{11,1... | collective-permute-start | bytes 147464 | tf_op jit(solution)/shard_map/ppermute | solution.py:18
  52.6 59.5 %all-to-all-start = ((f32[2,1,4,256]{2,0,1,3:T(2,128)}), f32[2,1,4,256]{2,0,1,3:T(2,128)S(1)}, u32[]{:S(2)}, u32[]{:S(2)}) async-start(f32[2,1,4,256]{2,0,1,3:T(2,128)} %copy.948), calls=%async_computation | async-start | bytes 524288 | tf_op jit(solution)/shard_map/all_to_all | solution.py:159
  107.8 25.7 %collective-permute-start.18 = (f32[2,1,4,12,256]{4,2,3,1,0:T(4,128)S(1)}, f32[2,1,4,12,256]{4,2,3,1,0:T(4,128)S(1)}, u32[]{:S(2)}, u32[]{:S(2)}) collective-permute-start(f32[2,1,4,12,256]{4,2,3,1,0:T(4,128)S(1)} %fusion.1104), channel_id=1, source_target_pairs={{1,0},{2,1},{3,2},{4,3},{5,4},{6,5},{7,6},{8,7},{9,8},{10,9},{11,1... | collective-permute-start | bytes 294920 | tf_op jit(solution)/shard_map/ppermute | solution.py:18
  109.1 24.4 %collective-permute-start.19 = (f32[2,1,4,12,256]{4,2,3,1,0:T(4,128)S(1)}, f32[2,1,4,12,256]{4,2,3,1,0:T(4,128)S(1)}, u32[]{:S(2)}, u32[]{:S(2)}) collective-permute-start(f32[2,1,4,12,256]{4,2,3,1,0:T(4,128)S(1)} %fusion.1104), channel_id=1, source_target_pairs={{0,1},{1,2},{2,3},{3,4},{4,5},{5,6},{6,7},{7,8},{8,9},{9,10},{10,1... | collective-permute-start | bytes 294920 | tf_op jit(solution)/shard_map/ppermute | solution.py:17
  113.6 14.4 %all-to-all-start.3 = ((f32[2,1,128,8]{3,0,1,2:T(2,128)}), f32[2,1,128,8]{3,0,1,2:T(2,128)S(1)}, u32[]{:S(2)}, u32[]{:S(2)}) async-start(f32[2,1,128,8]{3,0,1,2:T(2,128)} %copy.978), calls=%async_computation.3 | async-start | bytes 262144 | tf_op jit(solution)/shard_map/all_to_all | solution.py:131
  119.9 8.4 %collective-permute-start.7 = (f32[3,2,1,4,4,128]{5,4,3,2,1,0:T(4,128)S(1)}, f32[3,2,1,4,4,128]{5,4,3,2,1,0:T(4,128)S(1)}, u32[]{:S(2)}, u32[]{:S(2)}) collective-permute-start(f32[3,2,1,4,4,128]{5,4,3,2,1,0:T(4,128)S(1)} %get-tuple-element.243), channel_id=1, source_target_pairs={{1,0},{2,1},{3,2},{4,3},{5,4},{6,5},{7,6},{8,7},{9,8},{10,9},{11,1... | collective-permute-start | bytes 147464 | tf_op jit(solution)/shard_map/ppermute | solution.py:18
  129.1 9.5 %collective-permute-start.9 = (f32[3,2,1,4,4,128]{5,4,3,2,1,0:T(4,128)S(1)}, f32[3,2,1,4,4,128]{5,4,3,2,1,0:T(4,128)S(1)}, u32[]{:S(2)}, u32[]{:S(2)}) collective-permute-start(f32[3,2,1,4,4,128]{5,4,3,2,1,0:T(4,128)S(1)} %get-tuple-element.241), channel_id=1, source_target_pairs={{1,0},{2,1},{3,2},{4,3},{5,4},{6,5},{7,6},{8,7},{9,8},{10,9},{11,1... | collective-permute-start | bytes 147464 | tf_op jit(solution)/shard_map/ppermute | solution.py:18
  130.4 8.2 %collective-permute-start.8 = (f32[3,2,1,4,4,128]{5,4,3,2,1,0:T(4,128)S(1)}, f32[3,2,1,4,4,128]{5,4,3,2,1,0:T(4,128)S(1)}, u32[]{:S(2)}, u32[]{:S(2)}) collective-permute-start(f32[3,2,1,4,4,128]{5,4,3,2,1,0:T(4,128)S(1)} %get-tuple-element.240), channel_id=1, source_target_pairs={{0,1},{1,2},{2,3},{3,4},{4,5},{5,6},{6,7},{7,8},{8,9},{9,10},{10,1... | collective-permute-start | bytes 147464 | tf_op jit(solution)/shard_map/ppermute | solution.py:17
  142.7 59.0 %all-to-all-start.2 = ((f32[2,1,4,256]{2,0,1,3:T(2,128)}), f32[2,1,4,256]{2,0,1,3:T(2,128)S(1)}, u32[]{:S(2)}, u32[]{:S(2)}) async-start(f32[2,1,4,256]{2,0,1,3:T(2,128)} %copy.966), calls=%async_computation.2 | async-start | bytes 524288 | tf_op jit(solution)/shard_map/all_to_all | solution.py:159
  197.3 25.7 %collective-permute-start.24 = (f32[2,1,4,12,256]{4,2,3,1,0:T(4,128)S(1)}, f32[2,1,4,12,256]{4,2,3,1,0:T(4,128)S(1)}, u32[]{:S(2)}, u32[]{:S(2)}) collective-permute-start(f32[2,1,4,12,256]{4,2,3,1,0:T(4,128)S(1)} %fusion.1105), channel_id=1, source_target_pairs={{1,0},{2,1},{3,2},{4,3},{5,4},{6,5},{7,6},{8,7},{9,8},{10,9},{11,1... | collective-permute-start | bytes 294920 | tf_op jit(solution)/shard_map/ppermute | solution.py:18
  198.6 24.4 %collective-permute-start.25 = (f32[2,1,4,12,256]{4,2,3,1,0:T(4,128)S(1)}, f32[2,1,4,12,256]{4,2,3,1,0:T(4,128)S(1)}, u32[]{:S(2)}, u32[]{:S(2)}) collective-permute-start(f32[2,1,4,12,256]{4,2,3,1,0:T(4,128)S(1)} %fusion.1105), channel_id=1, source_target_pairs={{0,1},{1,2},{2,3},{3,4},{4,5},{5,6},{6,7},{7,8},{8,9},{9,10},{10,1... | collective-permute-start | bytes 294920 | tf_op jit(solution)/shard_map/ppermute | solution.py:17
  203.1 14.4 %all-to-all-start.5 = ((f32[2,1,128,8]{3,0,1,2:T(2,128)}), f32[2,1,128,8]{3,0,1,2:T(2,128)S(1)}, u32[]{:S(2)}, u32[]{:S(2)}) async-start(f32[2,1,128,8]{3,0,1,2:T(2,128)} %copy.989), calls=%async_computation.5 | async-start | bytes 262144 | tf_op jit(solution)/shard_map/all_to_all | solution.py:131
  209.4 8.4 %collective-permute-start.15 = (f32[3,2,1,4,4,128]{5,4,3,2,1,0:T(4,128)S(1)}, f32[3,2,1,4,4,128]{5,4,3,2,1,0:T(4,128)S(1)}, u32[]{:S(2)}, u32[]{:S(2)}) collective-permute-start(f32[3,2,1,4,4,128]{5,4,3,2,1,0:T(4,128)S(1)} %get-tuple-element.239), channel_id=1, source_target_pairs={{1,0},{2,1},{3,2},{4,3},{5,4},{6,5},{7,6},{8,7},{9,8},{10,9},{11,1... | collective-permute-start | bytes 147464 | tf_op jit(solution)/shard_map/ppermute | solution.py:18
  218.6 9.5 %collective-permute-start.17 = (f32[3,2,1,4,4,128]{5,4,3,2,1,0:T(4,128)S(1)}, f32[3,2,1,4,4,128]{5,4,3,2,1,0:T(4,128)S(1)}, u32[]{:S(2)}, u32[]{:S(2)}) collective-permute-start(f32[3,2,1,4,4,128]{5,4,3,2,1,0:T(4,128)S(1)} %get-tuple-element.237), channel_id=1, source_target_pairs={{1,0},{2,1},{3,2},{4,3},{5,4},{6,5},{7,6},{8,7},{9,8},{10,9},{11,1... | collective-permute-start | bytes 147464 | tf_op jit(solution)/shard_map/ppermute | solution.py:18
  232.2 59.0 %all-to-all-start.4 = ((f32[2,1,4,256]{2,0,1,3:T(2,128)}), f32[2,1,4,256]{2,0,1,3:T(2,128)S(1)}, u32[]{:S(2)}, u32[]{:S(2)}) async-start(f32[2,1,4,256]{2,0,1,3:T(2,128)} %copy.981), calls=%async_computation.4 | async-start | bytes 524288 | tf_op jit(solution)/shard_map/all_to_all | solution.py:159
  286.8 21.9 %collective-permute-start.28 = (f32[2,1,4,12,256]{4,2,3,1,0:T(4,128)S(1)}, f32[2,1,4,12,256]{4,2,3,1,0:T(4,128)S(1)}, u32[]{:S(2)}, u32[]{:S(2)}) collective-permute-start(f32[2,1,4,12,256]{4,2,3,1,0:T(4,128)S(1)} %fusion.1106), channel_id=1, source_target_pairs={{1,0},{2,1},{3,2},{4,3},{5,4},{6,5},{7,6},{8,7},{9,8},{10,9},{11,1... | collective-permute-start | bytes 294920 | tf_op jit(solution)/shard_map/ppermute | solution.py:18
  288.1 20.6 %collective-permute-start.29 = (f32[2,1,4,12,256]{4,2,3,1,0:T(4,128)S(1)}, f32[2,1,4,12,256]{4,2,3,1,0:T(4,128)S(1)}, u32[]{:S(2)}, u32[]{:S(2)}) collective-permute-start(f32[2,1,4,12,256]{4,2,3,1,0:T(4,128)S(1)} %fusion.1106), channel_id=1, source_target_pairs={{0,1},{1,2},{2,3},{3,4},{4,5},{5,6},{6,7},{7,8},{8,9},{9,10},{10,1... | collective-permute-start | bytes 294920 | tf_op jit(solution)/shard_map/ppermute | solution.py:17
  292.6 14.4 %all-to-all-start.6 = ((f32[2,1,128,8]{3,0,1,2:T(2,128)}), f32[2,1,128,8]{3,0,1,2:T(2,128)S(1)}, u32[]{:S(2)}, u32[]{:S(2)}) async-start(f32[2,1,128,8]{3,0,1,2:T(2,128)} %copy.992), calls=%async_computation.6 | async-start | bytes 262144 | tf_op jit(solution)/shard_map/all_to_all | solution.py:131
  298.9 8.4 %collective-permute-start.23 = (f32[3,2,1,4,4,128]{5,4,3,2,1,0:T(4,128)S(1)}, f32[3,2,1,4,4,128]{5,4,3,2,1,0:T(4,128)S(1)}, u32[]{:S(2)}, u32[]{:S(2)}) collective-permute-start(f32[3,2,1,4,4,128]{5,4,3,2,1,0:T(4,128)S(1)} %get-tuple-element.235), channel_id=1, source_target_pairs={{1,0},{2,1},{3,2},{4,3},{5,4},{6,5},{7,6},{8,7},{9,8},{10,9},{11,1... | collective-permute-start | bytes 147464 | tf_op jit(solution)/shard_map/ppermute | solution.py:18
  (26 other events, 152.1 us)
where the time goes:
time: 369 us; the launch traced here: 367 us
  blocking collectives  168 us (46%)
  starting transfers between devices  136 us (37%)
  waiting for transfers between devices  21 us (6%)
  other arithmetic  18.8 us (5%)
  local copies, waits for them, and re-layouts  14.5 us (4%)
  between operations  5.44 us (1%)
    psum x4, blocking collectives, on_device(): recorded = lax.psum(partial_record, 'gx')  168 us
    ppermute x16, starting transfers between devices, with_halo(): before = lax.ppermute(last, axis, up)  50.7 us
    all_to_all x3, starting transfers between devices, on_device(): lax.all_to_all(floor_pressure, 'gx', split_axis=3, concat_axis=2, tiled=T...  36.3 us
    all_to_all x4, starting transfers between devices, on_device(): lax.all_to_all(jnp.transpose(vel_z[:, :, :, 0, :], (0, 1, 3, 2)), 'gx', s...  28.3 us
    ppermute x16, starting transfers between devices, with_halo(): after = lax.ppermute(first, axis, down)  20.8 us
    all_to_all x4, waiting for transfers between devices, on_device(): lax.all_to_all(jnp.transpose(vel_z[:, :, :, 0, :], (0, 1, 3, 2)), 'gx', s...  14.8 us
  transfers between devices with their start and end apart: 39, of which 8 were waited for; matrix products, arithmetic and copies ran while one was open for 5% of the time, Pallas kernels for 0%

commit v1 on v0

--- a/solution.py
+++ b/solution.py
@@ -128,13 +128,10 @@
         vel_z = vel_z + TIME_STEP * solid_buoy * (
             stencil(stress_pad[2], 2, False) + derive(sig_yz, 4, False) + derive(sig_zz, 3, True)
         )
-        floor_velocity = lax.all_to_all(
-            jnp.transpose(vel_z[:, :, :, 0, :], (0, 1, 3, 2)),
-            "gx",
-            split_axis=2,
-            concat_axis=3,
-            tiled=True,
-        )
+        x = jnp.transpose(vel_z[:, :, :, 0, :], (0, 1, 3, 2))
+        pieces = jnp.split(x, lax.axis_size("gx"), axis=2)
+        incoming = lax.all_to_all(jnp.stack(pieces), "gx", 0, 0)
+        floor_velocity = jnp.concatenate(incoming, axis=3)
         flow_x = (flow_x - TIME_STEP * water_buoy * water_derive(pressure, 4, True)) * live
         flow_y = (flow_y - TIME_STEP * water_buoy * water_derive(pressure, 2, True)) * live
         flow_z = (

time: 369 us -> 456 us (1.24)
  local copies, waits for them, and re-layouts: 14.5 us -> 101 us
    unnamed x34 -> x161, local copies, waits for them, and re-layouts: 4.22 us -> 79.2 us
    split x0 -> x136, local copies, waits for them, and re-layouts: none -> 11.6 us  [on_device(): pieces = jnp.split(x, lax.axis_size('gx'), axis=2)]
    all_to_all x3, starting transfers between devices: 36.3 us -> 31.2 us  [on_device(): lax.all_to_all(floor_pressure, 'gx', split_axis=3, concat_axis=2, tiled=T...]
  transfers between devices with their start and end apart: 39 -> 39, of which waited for: 8 -> 8; matrix products, arithmetic and copies ran while one was open for 5% -> 23% of each run, Pallas kernels for 0% -> 0%
where the time goes in v1:
time: 456 us; the launch traced here: 453 us
  blocking collectives  168 us (37%)
  starting transfers between devices  134 us (29%)
  local copies, waits for them, and re-layouts  101 us (22%)
  waiting for transfers between devices  25.2 us (6%)
  other arithmetic  15.9 us (3%)
  between operations  5.63 us (1%)
    psum x4, blocking collectives, on_device(): recorded = lax.psum(partial_record, 'gx')  168 us
    unnamed x161, local copies, waits for them, and re-layouts  79.2 us
    ppermute x16, starting transfers between devices, with_halo(): before = lax.ppermute(last, axis, up)  52.3 us
    all_to_all x3, starting transfers between devices, on_device(): lax.all_to_all(floor_pressure, 'gx', split_axis=3, concat_axis=2, tiled=T...  31.2 us
    all_to_all x4, starting transfers between devices, on_device(): incoming = lax.all_to_all(jnp.stack(pieces), 'gx', 0, 0)  29.9 us
    ppermute x16, starting transfers between devices, with_halo(): after = lax.ppermute(first, axis, down)  20.8 us
    all_to_all x4, waiting for transfers between devices, on_device(): incoming = lax.all_to_all(jnp.stack(pieces), 'gx', 0, 0)  19.1 us
    split x136, local copies, waits for them, and re-layouts, on_device(): pieces = jnp.split(x, lax.axis_size('gx'), axis=2)  11.6 us
  transfers between devices with their start and end apart: 39, of which 8 were waited for; matrix products, arithmetic and copies ran while one was open for 23% of the time, Pallas kernels for 0%

profile of v1, /device:TPU:0, one launch (start us, length us, event | category | flops | bytes accessed | tf_op | source)
XLA Modules:
  0.0 453.2 jit_solution(6304260693991118387)
XLA Ops:
  2.8 3.0 collective-permute-start.11
  9.0 5.1 %collective-permute-start = (f32[3,2,1,4,4,128]{5,3,4,1,2,0:T(4,128)S(1)}, f32[3,2,1,4,4,128]{5,3,4,1,2,0:T(4,128)S(1)}, u32[]{:S(2)}, u32[]{:S(2)}) collective-permute-start(f32[3,2,1,4,4,128]{5,3,4,1,2,0:T(4,128)S(1)} %get-tuple-element.240), channel_id=1, source_target_pairs={{0,1},{1,2},{2,3},{3,4},{4,5},{5,6},{6,7},{7,8},{8,9},{9,10},{10,1... | collective-permute-start | bytes 147464 | tf_op jit(solution)/shard_map/ppermute | solution.py:17
  42.1 9.7 %all-to-all-start.1 = ((f32[32,2,1,4,8]{4,3,2,1,0:T(4,128)}), f32[32,2,1,4,8]{4,3,2,1,0:T(4,128)S(1)}, u32[]{:S(2)}, u32[]{:S(2)}) async-start(f32[32,2,1,4,8]{4,3,2,1,0:T(4,128)} %bitcast.268), calls=%async_computation.1 | async-start | bytes 262144 | tf_op jit(solution)/shard_map/all_to_all | solution.py:133
  56.7 3.4 all-to-all-done.1
  65.8 3.4 collective-permute-start.12
  74.5 12.3 %all-to-all-start = ((f32[2,1,4,256]{2,0,1,3:T(2,128)}), f32[2,1,4,256]{2,0,1,3:T(2,128)S(1)}, u32[]{:S(2)}, u32[]{:S(2)}) async-start(f32[2,1,4,256]{2,0,1,3:T(2,128)} %copy.2757), calls=%async_computation | async-start | bytes 524288 | tf_op jit(solution)/shard_map/all_to_all | solution.py:156
  87.3 40.5 %psum.28 = f32[1,128]{1,0:T(1,128)S(1)} all-reduce(f32[1,128]{1,0:T(1,128)S(1)} %fusion.7), channel_id=1, replica_groups=mesh['groups'=1,'gx'=32] {'gx'}, use_global_device_ids=true, to_apply=%region_2.3 | all-reduce | flops 128 | bytes 1024 | tf_op jit(solution)/shard_map/psum | solution.py:186
  130.8 3.0 collective-permute-start.19
  156.4 6.2 %all-to-all-start.3 = ((f32[32,2,1,4,8]{4,3,2,1,0:T(4,128)}), f32[32,2,1,4,8]{4,3,2,1,0:T(4,128)S(1)}, u32[]{:S(2)}, u32[]{:S(2)}) async-start(f32[32,2,1,4,8]{4,3,2,1,0:T(4,128)} %bitcast.413), calls=%async_computation.3 | async-start | bytes 262144 | tf_op jit(solution)/shard_map/all_to_all | solution.py:133
  167.0 3.8 all-to-all-done.3
  176.4 3.4 collective-permute-start.20
  185.2 11.9 %all-to-all-start.2 = ((f32[2,1,4,256]{2,0,1,3:T(2,128)}), f32[2,1,4,256]{2,0,1,3:T(2,128)S(1)}, u32[]{:S(2)}, u32[]{:S(2)}) async-start(f32[2,1,4,256]{2,0,1,3:T(2,128)} %copy.2873), calls=%async_computation.2 | async-start | bytes 524288 | tf_op jit(solution)/shard_map/all_to_all | solution.py:156
  197.6 40.5 %psum.29 = f32[1,128]{1,0:T(1,128)S(1)} all-reduce(f32[1,128]{1,0:T(1,128)S(1)} %fusion.5), channel_id=1, replica_groups=mesh['groups'=1,'gx'=32] {'gx'}, use_global_device_ids=true, to_apply=%region_6.7 | all-reduce | flops 128 | bytes 1024 | tf_op jit(solution)/shard_map/psum | solution.py:186
  241.1 3.2 collective-permute-start.25
  246.5 4.4 collective-permute-start.14
  272.6 7.8 %all-to-all-start.5 = ((f32[32,2,1,4,8]{4,3,2,1,0:T(4,128)}), f32[32,2,1,4,8]{4,3,2,1,0:T(4,128)S(1)}, u32[]{:S(2)}, u32[]{:S(2)}) async-start(f32[32,2,1,4,8]{4,3,2,1,0:T(4,128)} %bitcast.503), calls=%async_computation.5 | async-start | bytes 262144 | tf_op jit(solution)/shard_map/all_to_all | solution.py:133
  280.6 8.1 %all-to-all-done.5 = f32[32,2,1,4,8]{4,3,2,1,0:T(4,128)S(1)} async-done(((f32[32,2,1,4,8]{4,3,2,1,0:T(4,128)}), f32[32,2,1,4,8]{4,3,2,1,0:T(4,128)S(1)}, u32[]{:S(2)}, u32[]{:S(2)}) %all-to-all-start.5) | async-done | bytes 8224 | tf_op jit(solution)/shard_map/all_to_all | solution.py:133
  294.3 3.4 collective-permute-start.26
  303.0 7.0 %all-to-all-start.4 = ((f32[2,1,4,256]{2,0,1,3:T(2,128)}), f32[2,1,4,256]{2,0,1,3:T(2,128)S(1)}, u32[]{:S(2)}, u32[]{:S(2)}) async-start(f32[2,1,4,256]{2,0,1,3:T(2,128)} %copy.2993), calls=%async_computation.4 | async-start | bytes 524288 | tf_op jit(solution)/shard_map/all_to_all | solution.py:156
  310.5 40.5 %psum.30 = f32[1,128]{1,0:T(1,128)S(1)} all-reduce(f32[1,128]{1,0:T(1,128)S(1)} %fusion.3), channel_id=1, replica_groups=mesh['groups'=1,'gx'=32] {'gx'}, use_global_device_ids=true, to_apply=%region_10.11 | all-reduce | flops 128 | bytes 1024 | tf_op jit(solution)/shard_map/psum | solution.py:186
  354.0 3.0 collective-permute-start.29
  379.6 6.2 %all-to-all-start.6 = ((f32[32,2,1,4,8]{4,3,2,1,0:T(4,128)}), f32[32,2,1,4,8]{4,3,2,1,0:T(4,128)S(1)}, u32[]{:S(2)}, u32[]{:S(2)}) async-start(f32[32,2,1,4,8]{4,3,2,1,0:T(4,128)} %bitcast.546), calls=%async_computation.6 | async-start | bytes 262144 | tf_op jit(solution)/shard_map/all_to_all | solution.py:133
  390.3 3.8 all-to-all-done.6
  403.1 46.5 %psum.31 = f32[1,128]{1,0:T(1,128)S(1)} all-reduce(f32[1,128]{1,0:T(1,128)S(1)} %fusion.1), channel_id=1, replica_groups=mesh['groups'=1,'gx'=32] {'gx'}, use_global_device_ids=true, to_apply=%region_13.14 | all-reduce | flops 128 | bytes 1024 | tf_op jit(solution)/shard_map/psum | solution.py:186
  (518 shorter events, 167.5 us)
Async XLA Ops:
  1.5 63.7 %collective-permute-start.10 = (f32[2,1,4,12,256]{4,2,3,1,0:T(4,128)S(1)}, f32[2,1,4,12,256]{4,2,3,1,0:T(4,128)S(1)}, u32[]{:S(2)}, u32[]{:S(2)}) collective-permute-start(f32[2,1,4,12,256]{4,2,3,1,0:T(4,128)S(1)} %slice_bitcast_fusion.3), channel_id=1, source_target_pairs={{1,0},{2,1},{3,2},{4,3},{5,4},{6,5},{7,6},{8,7},{9,8},{10,9},{11,1... | collective-permute-start | bytes 294920 | tf_op jit(solution)/shard_map/ppermute | solution.py:18
  2.8 62.5 %collective-permute-start.11 = (f32[2,1,4,12,256]{4,2,3,1,0:T(4,128)S(1)}, f32[2,1,4,12,256]{4,2,3,1,0:T(4,128)S(1)}, u32[]{:S(2)}, u32[]{:S(2)}) collective-permute-start(f32[2,1,4,12,256]{4,2,3,1,0:T(4,128)S(1)} %slice_bitcast_fusion.3), channel_id=1, source_target_pairs={{0,1},{1,2},{2,3},{3,4},{4,5},{5,6},{6,7},{7,8},{8,9},{9,10},{10,1... | collective-permute-start | bytes 294920 | tf_op jit(solution)/shard_map/ppermute | solution.py:17
  7.7 12.3 %collective-permute-start.1 = (f32[3,2,1,4,4,128]{5,3,4,1,2,0:T(4,128)S(1)}, f32[3,2,1,4,4,128]{5,3,4,1,2,0:T(4,128)S(1)}, u32[]{:S(2)}, u32[]{:S(2)}) collective-permute-start(f32[3,2,1,4,4,128]{5,3,4,1,2,0:T(4,128)S(1)} %get-tuple-element.241), channel_id=1, source_target_pairs={{1,0},{2,1},{3,2},{4,3},{5,4},{6,5},{7,6},{8,7},{9,8},{10,9},{11,1... | collective-permute-start | bytes 147464 | tf_op jit(solution)/shard_map/ppermute | solution.py:18
  9.0 11.0 %collective-permute-start = (f32[3,2,1,4,4,128]{5,3,4,1,2,0:T(4,128)S(1)}, f32[3,2,1,4,4,128]{5,3,4,1,2,0:T(4,128)S(1)}, u32[]{:S(2)}, u32[]{:S(2)}) collective-permute-start(f32[3,2,1,4,4,128]{5,3,4,1,2,0:T(4,128)S(1)} %get-tuple-element.240), channel_id=1, source_target_pairs={{0,1},{1,2},{2,3},{3,4},{4,5},{5,6},{6,7},{7,8},{8,9},{9,10},{10,1... | collective-permute-start | bytes 147464 | tf_op jit(solution)/shard_map/ppermute | solution.py:17
  42.1 18.0 %all-to-all-start.1 = ((f32[32,2,1,4,8]{4,3,2,1,0:T(4,128)}), f32[32,2,1,4,8]{4,3,2,1,0:T(4,128)S(1)}, u32[]{:S(2)}, u32[]{:S(2)}) async-start(f32[32,2,1,4,8]{4,3,2,1,0:T(4,128)} %bitcast.268), calls=%async_computation.1 | async-start | bytes 262144 | tf_op jit(solution)/shard_map/all_to_all | solution.py:133
  60.9 9.5 %collective-permute-start.5 = (f32[3,2,1,4,4,128]{5,3,4,1,2,0:T(4,128)S(1)}, f32[3,2,1,4,4,128]{5,3,4,1,2,0:T(4,128)S(1)}, u32[]{:S(2)}, u32[]{:S(2)}) collective-permute-start(f32[3,2,1,4,4,128]{5,3,4,1,2,0:T(4,128)S(1)} %get-tuple-element.237), channel_id=1, source_target_pairs={{1,0},{2,1},{3,2},{4,3},{5,4},{6,5},{7,6},{8,7},{9,8},{10,9},{11,1... | collective-permute-start | bytes 147464 | tf_op jit(solution)/shard_map/ppermute | solution.py:18
  74.5 59.4 %all-to-all-start = ((f32[2,1,4,256]{2,0,1,3:T(2,128)}), f32[2,1,4,256]{2,0,1,3:T(2,128)S(1)}, u32[]{:S(2)}, u32[]{:S(2)}) async-start(f32[2,1,4,256]{2,0,1,3:T(2,128)} %copy.2757), calls=%async_computation | async-start | bytes 524288 | tf_op jit(solution)/shard_map/all_to_all | solution.py:156
  129.5 46.4 %collective-permute-start.18 = (f32[2,1,4,12,256]{4,2,3,1,0:T(4,128)S(1)}, f32[2,1,4,12,256]{4,2,3,1,0:T(4,128)S(1)}, u32[]{:S(2)}, u32[]{:S(2)}) collective-permute-start(f32[2,1,4,12,256]{4,2,3,1,0:T(4,128)S(1)} %fusion.861), channel_id=1, source_target_pairs={{1,0},{2,1},{3,2},{4,3},{5,4},{6,5},{7,6},{8,7},{9,8},{10,9},{11,1... | collective-permute-start | bytes 294920 | tf_op jit(solution)/shard_map/ppermute | solution.py:18
  130.8 45.1 %collective-permute-start.19 = (f32[2,1,4,12,256]{4,2,3,1,0:T(4,128)S(1)}, f32[2,1,4,12,256]{4,2,3,1,0:T(4,128)S(1)}, u32[]{:S(2)}, u32[]{:S(2)}) collective-permute-start(f32[2,1,4,12,256]{4,2,3,1,0:T(4,128)S(1)} %fusion.861), channel_id=1, source_target_pairs={{0,1},{1,2},{2,3},{3,4},{4,5},{5,6},{6,7},{7,8},{8,9},{9,10},{10,1... | collective-permute-start | bytes 294920 | tf_op jit(solution)/shard_map/ppermute | solution.py:17
  156.4 14.4 %all-to-all-start.3 = ((f32[32,2,1,4,8]{4,3,2,1,0:T(4,128)}), f32[32,2,1,4,8]{4,3,2,1,0:T(4,128)S(1)}, u32[]{:S(2)}, u32[]{:S(2)}) async-start(f32[32,2,1,4,8]{4,3,2,1,0:T(4,128)} %bitcast.413), calls=%async_computation.3 | async-start | bytes 262144 | tf_op jit(solution)/shard_map/all_to_all | solution.py:133
  162.6 8.4 %collective-permute-start.7 = (f32[3,2,1,4,4,128]{5,3,4,1,2,0:T(4,128)S(1)}, f32[3,2,1,4,4,128]{5,3,4,1,2,0:T(4,128)S(1)}, u32[]{:S(2)}, u32[]{:S(2)}) collective-permute-start(f32[3,2,1,4,4,128]{5,3,4,1,2,0:T(4,128)S(1)} %get-tuple-element.235), channel_id=1, source_target_pairs={{1,0},{2,1},{3,2},{4,3},{5,4},{6,5},{7,6},{8,7},{9,8},{10,9},{11,1... | collective-permute-start | bytes 147464 | tf_op jit(solution)/shard_map/ppermute | solution.py:18
  171.6 9.5 %collective-permute-start.9 = (f32[3,2,1,4,4,128]{5,3,4,1,2,0:T(4,128)S(1)}, f32[3,2,1,4,4,128]{5,3,4,1,2,0:T(4,128)S(1)}, u32[]{:S(2)}, u32[]{:S(2)}) collective-permute-start(f32[3,2,1,4,4,128]{5,3,4,1,2,0:T(4,128)S(1)} %get-tuple-element.233), channel_id=1, source_target_pairs={{1,0},{2,1},{3,2},{4,3},{5,4},{6,5},{7,6},{8,7},{9,8},{10,9},{11,1... | collective-permute-start | bytes 147464 | tf_op jit(solution)/shard_map/ppermute | solution.py:18
  185.2 59.1 %all-to-all-start.2 = ((f32[2,1,4,256]{2,0,1,3:T(2,128)}), f32[2,1,4,256]{2,0,1,3:T(2,128)S(1)}, u32[]{:S(2)}, u32[]{:S(2)}) async-start(f32[2,1,4,256]{2,0,1,3:T(2,128)} %copy.2873), calls=%async_computation.2 | async-start | bytes 524288 | tf_op jit(solution)/shard_map/all_to_all | solution.py:156
  239.8 54.0 %collective-permute-start.24 = (f32[2,1,4,12,256]{4,2,3,1,0:T(4,128)S(1)}, f32[2,1,4,12,256]{4,2,3,1,0:T(4,128)S(1)}, u32[]{:S(2)}, u32[]{:S(2)}) collective-permute-start(f32[2,1,4,12,256]{4,2,3,1,0:T(4,128)S(1)} %fusion.862), channel_id=1, source_target_pairs={{1,0},{2,1},{3,2},{4,3},{5,4},{6,5},{7,6},{8,7},{9,8},{10,9},{11,1... | collective-permute-start | bytes 294920 | tf_op jit(solution)/shard_map/ppermute | solution.py:18
  241.1 52.7 %collective-permute-start.25 = (f32[2,1,4,12,256]{4,2,3,1,0:T(4,128)S(1)}, f32[2,1,4,12,256]{4,2,3,1,0:T(4,128)S(1)}, u32[]{:S(2)}, u32[]{:S(2)}) collective-permute-start(f32[2,1,4,12,256]{4,2,3,1,0:T(4,128)S(1)} %fusion.862), channel_id=1, source_target_pairs={{0,1},{1,2},{2,3},{3,4},{4,5},{5,6},{6,7},{7,8},{8,9},{9,10},{10,1... | collective-permute-start | bytes 294920 | tf_op jit(solution)/shard_map/ppermute | solution.py:17
  245.2 43.8 %collective-permute-start.15 = (f32[3,2,1,4,4,128]{5,3,4,1,2,0:T(4,128)S(1)}, f32[3,2,1,4,4,128]{5,3,4,1,2,0:T(4,128)S(1)}, u32[]{:S(2)}, u32[]{:S(2)}) collective-permute-start(f32[3,2,1,4,4,128]{5,3,4,1,2,0:T(4,128)S(1)} %get-tuple-element.231), channel_id=1, source_target_pairs={{1,0},{2,1},{3,2},{4,3},{5,4},{6,5},{7,6},{8,7},{9,8},{10,9},{11,1... | collective-permute-start | bytes 147464 | tf_op jit(solution)/shard_map/ppermute | solution.py:18
  246.5 42.5 %collective-permute-start.14 = (f32[3,2,1,4,4,128]{5,3,4,1,2,0:T(4,128)S(1)}, f32[3,2,1,4,4,128]{5,3,4,1,2,0:T(4,128)S(1)}, u32[]{:S(2)}, u32[]{:S(2)}) collective-permute-start(f32[3,2,1,4,4,128]{5,3,4,1,2,0:T(4,128)S(1)} %get-tuple-element.230), channel_id=1, source_target_pairs={{0,1},{1,2},{2,3},{3,4},{4,5},{5,6},{6,7},{7,8},{8,9},{9,10},{10,1... | collective-permute-start | bytes 147464 | tf_op jit(solution)/shard_map/ppermute | solution.py:17
  272.6 16.1 %all-to-all-start.5 = ((f32[32,2,1,4,8]{4,3,2,1,0:T(4,128)}), f32[32,2,1,4,8]{4,3,2,1,0:T(4,128)S(1)}, u32[]{:S(2)}, u32[]{:S(2)}) async-start(f32[32,2,1,4,8]{4,3,2,1,0:T(4,128)} %bitcast.503), calls=%async_computation.5 | async-start | bytes 262144 | tf_op jit(solution)/shard_map/all_to_all | solution.py:133
  289.4 9.5 %collective-permute-start.17 = (f32[3,2,1,4,4,128]{5,3,4,1,2,0:T(4,128)S(1)}, f32[3,2,1,4,4,128]{5,3,4,1,2,0:T(4,128)S(1)}, u32[]{:S(2)}, u32[]{:S(2)}) collective-permute-start(f32[3,2,1,4,4,128]{5,3,4,1,2,0:T(4,128)S(1)} %get-tuple-element.229), channel_id=1, source_target_pairs={{1,0},{2,1},{3,2},{4,3},{5,4},{6,5},{7,6},{8,7},{9,8},{10,9},{11,1... | collective-permute-start | bytes 147464 | tf_op jit(solution)/shard_map/ppermute | solution.py:18
  303.0 54.0 %all-to-all-start.4 = ((f32[2,1,4,256]{2,0,1,3:T(2,128)}), f32[2,1,4,256]{2,0,1,3:T(2,128)S(1)}, u32[]{:S(2)}, u32[]{:S(2)}) async-start(f32[2,1,4,256]{2,0,1,3:T(2,128)} %copy.2993), calls=%async_computation.4 | async-start | bytes 524288 | tf_op jit(solution)/shard_map/all_to_all | solution.py:156
  352.7 42.0 %collective-permute-start.28 = (f32[2,1,4,12,256]{4,2,3,1,0:T(4,128)S(1)}, f32[2,1,4,12,256]{4,2,3,1,0:T(4,128)S(1)}, u32[]{:S(2)}, u32[]{:S(2)}) collective-permute-start(f32[2,1,4,12,256]{4,2,3,1,0:T(4,128)S(1)} %fusion.863), channel_id=1, source_target_pairs={{1,0},{2,1},{3,2},{4,3},{5,4},{6,5},{7,6},{8,7},{9,8},{10,9},{11,1... | collective-permute-start | bytes 294920 | tf_op jit(solution)/shard_map/ppermute | solution.py:18
  354.0 40.7 %collective-permute-start.29 = (f32[2,1,4,12,256]{4,2,3,1,0:T(4,128)S(1)}, f32[2,1,4,12,256]{4,2,3,1,0:T(4,128)S(1)}, u32[]{:S(2)}, u32[]{:S(2)}) collective-permute-start(f32[2,1,4,12,256]{4,2,3,1,0:T(4,128)S(1)} %fusion.863), channel_id=1, source_target_pairs={{0,1},{1,2},{2,3},{3,4},{4,5},{5,6},{6,7},{7,8},{8,9},{9,10},{10,1... | collective-permute-start | bytes 294920 | tf_op jit(solution)/shard_map/ppermute | solution.py:17
  379.6 14.4 %all-to-all-start.6 = ((f32[32,2,1,4,8]{4,3,2,1,0:T(4,128)}), f32[32,2,1,4,8]{4,3,2,1,0:T(4,128)S(1)}, u32[]{:S(2)}, u32[]{:S(2)}) async-start(f32[32,2,1,4,8]{4,3,2,1,0:T(4,128)} %bitcast.546), calls=%async_computation.6 | async-start | bytes 262144 | tf_op jit(solution)/shard_map/all_to_all | solution.py:133
  385.9 8.4 %collective-permute-start.23 = (f32[3,2,1,4,4,128]{5,3,4,1,2,0:T(4,128)S(1)}, f32[3,2,1,4,4,128]{5,3,4,1,2,0:T(4,128)S(1)}, u32[]{:S(2)}, u32[]{:S(2)}) collective-permute-start(f32[3,2,1,4,4,128]{5,3,4,1,2,0:T(4,128)S(1)} %get-tuple-element.227), channel_id=1, source_target_pairs={{1,0},{2,1},{3,2},{4,3},{5,4},{6,5},{7,6},{8,7},{9,8},{10,9},{11,1... | collective-permute-start | bytes 147464 | tf_op jit(solution)/shard_map/ppermute | solution.py:18
  (26 other events, 148.4 us)
